TPU v7x, 256 devices: a whole 4x4x8 slice. The times are simulated.
256 devices in a mesh: leaf: 4 (over z_hi), row: 8 (over z_lo, y), col: 8 (over x, core).
Axes of the slice: x: 4, y: 4, z: 8 (z_hi: 4, z_lo: 2; z = z_hi * 2 + z_lo), core: 2. Of those that a mesh axis runs over, the one named last changes fastest.
Arguments:
- lanczos_low: float32 [4, 8, 8, 128, 256], P('leaf', 'col', 'row'), may hold values from -6 to 6
- lanczos_mid: float32 [4, 8, 8, 96, 256], P('leaf', 'col', 'row'), may hold values from -6 to 6
- lanczos_top: float32 [4, 8, 8, 64, 256], P('leaf', 'col', 'row'), may hold values from -6 to 6
- pivot_low: bfloat16 [4, 8192, 8192], P('leaf', 'row', 'col'), as said below
- update_low: bfloat16 [4, 8192, 8192], P('leaf', 'row', 'col'), may hold values from -0.0625 to 0.0625
- pivot_mid: bfloat16 [12288, 24576], P('row', ('leaf', 'col'))
- update_mid: bfloat16 [12288, 16384], P('row', ('leaf', 'col')), may hold values from -0.0546875 to 0.0546875
- pivot_top: bfloat16 [16384, 16384], P('row', ('leaf', 'col'))
- rows_low: int32 [4, 8, 8, 2, 64], P('leaf', 'col', 'row'), may hold values from 0 to 20479, as said below
- rows_mid: int32 [4, 8, 8, 4, 16], P('leaf', 'col', 'row'), may hold values from 0 to 16383, as said below
Outputs:
- solved_low: float32 [4, 8, 8, 128, 256], P('leaf', 'col', 'row')
- solved_mid: float32 [4, 8, 8, 96, 256], P('leaf', 'col', 'row')
- solved_top: float32 [4, 8, 8, 64, 256], P('leaf', 'col', 'row')
Inputs may be any that keep to these rules, and one draw needn't show every extreme that they name: rows_low[2h + a, c, r, s, t] over t are distinct rows of front h, all among pivot rows a 6144 + (c * 8 + r) * 96 + k (0 <= k < 96) and update rows 12288 + a 4096 + (c * 8 + r) * 64 + k (0 <= k < 64); for s = 0 they include the first of those pivot rows and the last of those update rows. rows_mid[q, c, r, 2h + s, t] over s and t are distinct root rows q * 4096 + (c * 8 + r) * 64 + k (0 <= k < 64); for h = 0 they include the first and the last of them. pivot_low, pivot_mid's two square halves and pivot_top are lower triangular.
All inputs are finite; a program needn't handle non-finite values.
Results may differ from a plain program's by a relative error of at most 0.023.
Values may be sent and summed in bfloat16 or wider, within the bound.
No kernel may reach another device: no remote copies, remote signals or barrier semaphores. Data moves between devices by JAX's collectives and lax.ppermute only.
A program may use at most 64 MiB of HBM per device.

v0:
```python
import jax
import jax.numpy as jnp
from jax import lax
from jax.sharding import PartitionSpec as P

P1 = 12288


def from_partner(block, axis, bit):
    count = lax.axis_size(axis)
    route = []
    for low in range(count):
        high = low | 1 << bit
        if high != low and high < count:
            route += [(low, high), (high, low)]
    return lax.ppermute(block, axis, route)


def partner(block_data, leaf_bit):
    return from_partner(block_data.astype(jnp.bfloat16), "leaf", leaf_bit).astype(block_data.dtype)


def forward_apply(matrix, vector, leaf_bits):
    gathered = lax.all_gather(vector, "row", axis=0, tiled=True)
    result = lax.psum_scatter(
        jnp.dot(matrix, gathered, preferred_element_type=jnp.float32),
        "col",
        scatter_dimension=0,
        tiled=True,
    )
    for leaf_bit in leaf_bits:
        result = result + partner(result, leaf_bit)
    return result


def reverse_apply(matrix, vector):
    gathered = lax.all_gather(vector, "col", axis=0, tiled=True)
    return lax.psum_scatter(
        lax.dot_general(
            matrix, gathered, (((0,), (0,)), ((), ())), preferred_element_type=jnp.float32
        ).astype(jnp.bfloat16),
        "row",
        scatter_dimension=0,
        tiled=True,
    ).astype(jnp.float32)


def parent_slot(parent_rows, pivot_local, update_local):
    return jnp.where(
        parent_rows < P1, parent_rows % pivot_local, pivot_local + (parent_rows - P1) % update_local
    )


def pick_span(spans, index_value):
    return lax.dynamic_index_in_dim(spans, index_value, 0, keepdims=False)


def body(
    lanczos_low,
    lanczos_mid,
    lanczos_top,
    pivot_low,
    update_low,
    pivot_mid,
    update_mid,
    pivot_top,
    rows_low,
    rows_mid,
):
    rhs_width = lanczos_low.shape[-1]
    low_in = lanczos_low.reshape(-1, rhs_width)
    mid_in = lanczos_mid.reshape(-1, rhs_width)
    top_in = lanczos_top.reshape(-1, rhs_width)
    pivot_local_low = pivot_low[0]
    update_local_low = update_low[0]
    pivot_local = mid_in.shape[0]
    update_local = update_mid.shape[1] // lax.axis_size("row")
    top_local = top_in.shape[0]
    group_id = lax.axis_index("leaf")
    own_half = group_id % 2
    child_slots = parent_slot(rows_low.reshape(2, -1), pivot_local, update_local)
    root_slots = rows_mid.reshape(4, -1) % top_local
    source_order = jnp.bitwise_xor(group_id, jnp.arange(4, dtype=jnp.int32))
    source_slots = jnp.take(root_slots, source_order, axis=0).reshape(-1)
    own_slots = pick_span(child_slots, own_half)
    other_slots = pick_span(child_slots, 1 - own_half)
    low_y = forward_apply(pivot_local_low, low_in.astype(jnp.bfloat16), ())
    low_c = reverse_apply(update_local_low, low_y.astype(jnp.bfloat16)).reshape(2, -1, rhs_width)
    own_part = pick_span(low_c, own_half)
    came_part = partner(pick_span(low_c, 1 - own_half), 0)
    front_rows = jnp.concatenate([mid_in, jnp.zeros((update_local, rhs_width), mid_in.dtype)], 0)
    front_rows = front_rows.at[own_slots].add(-own_part).at[other_slots].add(-came_part)
    mid_y = forward_apply(pivot_mid, front_rows[:pivot_local].astype(jnp.bfloat16), (0,))
    mid_c = front_rows[pivot_local:] - reverse_apply(update_mid, mid_y.astype(jnp.bfloat16))
    spans = mid_c.reshape(4, -1, rhs_width)
    kept_spans = jnp.stack(
        [pick_span(spans, group_id), pick_span(spans, jnp.bitwise_xor(group_id, 2))]
    )
    moved_spans = partner(
        jnp.stack(
            [
                pick_span(spans, jnp.bitwise_xor(group_id, 1)),
                pick_span(spans, jnp.bitwise_xor(group_id, 3)),
            ]
        ),
        0,
    )
    second = partner(jnp.stack([kept_spans[1], moved_spans[1]]), 1)
    arrived = jnp.stack([kept_spans[0], moved_spans[0], second[0], second[1]]).reshape(
        -1, rhs_width
    )
    top_front = top_in.at[source_slots].add(arrived)
    top_y = forward_apply(pivot_top, top_front.astype(jnp.bfloat16), (0, 1))
    top_x = reverse_apply(pivot_top, top_y.astype(jnp.bfloat16))
    asked_rows = top_x[source_slots].reshape(4, -1, rhs_width)
    back_one = partner(jnp.stack([asked_rows[2], asked_rows[3]]), 1)
    back_zero = partner(jnp.stack([asked_rows[1], back_one[1]]), 0)
    by_root = jnp.stack([asked_rows[0], back_zero[0], back_one[0], back_zero[1]])
    mid_above = jnp.take(by_root, source_order, axis=0).reshape(-1, rhs_width)
    mid_sum = forward_apply(update_mid, mid_above.astype(jnp.bfloat16), (0,))
    mid_x = reverse_apply(pivot_mid, (mid_y - mid_sum).astype(jnp.bfloat16))
    front_values = jnp.concatenate([mid_x, mid_above], 0)
    own_rows = front_values[own_slots]
    got_rows = partner(front_values[other_slots], 0)
    low_above = jnp.where(
        own_half == 0,
        jnp.concatenate([own_rows, got_rows], 0),
        jnp.concatenate([got_rows, own_rows], 0),
    )
    low_sum = forward_apply(update_local_low, low_above.astype(jnp.bfloat16), ())
    low_x = reverse_apply(pivot_local_low, (low_y - low_sum).astype(jnp.bfloat16))
    return (
        low_x.reshape(lanczos_low.shape),
        mid_x.reshape(lanczos_mid.shape),
        top_x.reshape(lanczos_top.shape),
    )


def solution(mesh):
    return jax.shard_map(
        body,
        mesh=mesh,
        in_specs=(
            P("leaf", "col", "row", None, None),
            P("leaf", "col", "row", None, None),
            P("leaf", "col", "row", None, None),
            P("leaf", "row", "col"),
            P("leaf", "row", "col"),
            P("row", ("leaf", "col")),
            P("row", ("leaf", "col")),
            P("row", ("leaf", "col")),
            P("leaf", "col", "row", None, None),
            P("leaf", "col", "row", None, None),
        ),
        out_specs=(
            P("leaf", "col", "row", None, None),
            P("leaf", "col", "row", None, None),
            P("leaf", "col", "row", None, None),
        ),
        check_vma=False,
    )
```

profile of v0, /device:TPU:2, one launch (start us, length us, event | category | flops | bytes accessed | tf_op | source)
XLA Modules:
  0.0 739.1 jit_solution(14551251856389087296)
XLA Ops:
  7.2 1.1 convert_element_type.123
  8.3 29.8 %all-gather = bf16[1,1,1,1024,256]{4,3,2,1,0:T(8,128)(2,1)S(1)} all-gather(bf16[1,1,1,128,256]{4,3,2,1,0:T(8,128)(2,1)S(1)} %convert_element_type.123), channel_id=2, replica_groups=mesh['leaf'=4,'row'=8,'col'=8] {'row'}, dimensions={3}, use_global_device_ids=true | all-gather | bytes 589824 | tf_op jit(solution)/shard_map/all_gather | solution.py:24
  38.1 3.3 fusion.6
  41.5 33.6 %reduce-scatter.25.cloned.1.call-done = f32[128,256]{1,0:T(8,128)} async-done(((f32[1024,256]{1,0:T(8,128)}), f32[128,256]{1,0:T(8,128)}) %reduce-scatter.25.cloned.1.call-update) | async-done | bytes 131088 | tf_op jit(solution)/shard_map/reduce_scatter | solution.py:25
  76.0 13.8 %all_gather.31 = bf16[1024,256]{1,0:T(8,128)(2,1)S(1)} all-gather(bf16[128,256]{1,0:T(8,128)(2,1)S(1)} %convert_element_type.125), channel_id=1, replica_groups=mesh['leaf'=4,'row'=8,'col'=8] {'col'}, dimensions={0}, use_global_device_ids=true | all-gather | bytes 589824 | tf_op jit(solution)/shard_map/all_gather | solution.py:37
  89.8 2.3 fusion.17
  92.1 1.0 copy.43
  93.3 42.9 %reduce-scatter.31.cloned.1.call-done = bf16[128,256]{1,0:T(8,128)(2,1)} async-done(((bf16[1024,256]{1,0:T(8,128)(2,1)}), bf16[128,256]{1,0:T(8,128)(2,1)}) %reduce-scatter.31.cloned.1.call-update) | async-done | bytes 65552 | tf_op jit(solution)/shard_map/reduce_scatter | solution.py:38
  137.1 2.8 collective-permute-start
  139.9 1.0 scatter_custom_fusion
  140.9 1.4 collective-permute-done
  142.3 1.0 scatter_custom_fusion.1
  143.3 28.8 %all_gather.32 = bf16[768,256]{1,0:T(8,128)(2,1)S(1)} all-gather(bf16[96,256]{1,0:T(8,128)(2,1)S(1)} %slice.113), channel_id=1, replica_groups=mesh['leaf'=4,'row'=8,'col'=8] {'row'}, dimensions={0}, use_global_device_ids=true | all-gather | bytes 442368 | tf_op jit(solution)/shard_map/all_gather | solution.py:24
  172.2 2.0 convolution_bitcast_fusion.2
  174.1 3.0 copy.45
  177.3 31.0 %reduce-scatter.33.cloned.1.call-done = f32[192,256]{1,0:T(8,128)} async-done(((f32[1536,256]{1,0:T(8,128)}), f32[192,256]{1,0:T(8,128)}) %reduce-scatter.33.cloned.1.call-update) | async-done | bytes 196624
  208.3 1.1 copy.46
  209.3 2.6 collective-permute-start.1
  212.0 5.8 collective-permute-done.1
  217.9 14.6 %all_gather.33 = bf16[1536,256]{1,0:T(8,128)(2,1)S(1)} all-gather(bf16[192,256]{1,0:T(8,128)(2,1)S(1)} %copy.35), channel_id=1, replica_groups=mesh['leaf'=4,'row'=8,'col'=8] {'col'}, dimensions={0}, use_global_device_ids=true | all-gather | bytes 884736 | tf_op jit(solution)/shard_map/all_gather | solution.py:37
  232.5 2.0 fusion.24
  236.2 41.2 %reduce-scatter.35.cloned.1.call-done = bf16[64,256]{1,0:T(8,128)(2,1)} async-done(((bf16[512,256]{1,0:T(8,128)(2,1)}), bf16[64,256]{1,0:T(8,128)(2,1)}) %reduce-scatter.35.cloned.1.call-update) | async-done | bytes 32784 | tf_op jit(solution)/shard_map/reduce_scatter | solution.py:38
  278.2 2.6 collective-permute-start.2
  280.8 2.2 collective-permute-done.2
  283.0 4.8 collective-permute-start.3
  287.8 2.9 collective-permute-done.3
  290.7 1.0 scatter_fusion
  291.8 28.4 %all_gather.34 = bf16[512,256]{1,0:T(8,128)(2,1)S(1)} all-gather(bf16[64,256]{1,0:T(8,128)(2,1)S(1)} %convert_element_type.138), channel_id=1, replica_groups=mesh['leaf'=4,'row'=8,'col'=8] {'row'}, dimensions={0}, use_global_device_ids=true | all-gather | bytes 294912 | tf_op jit(solution)/shard_map/all_gather | solution.py:24
  320.1 3.7 convolution_bitcast_fusion.1
  323.9 32.4 %reduce-scatter.27.cloned.1.call-done = f32[256,256]{0,1:T(8,128)} async-done(((f32[2048,256]{0,1:T(8,128)}), f32[256,256]{0,1:T(8,128)}) %reduce-scatter.27.cloned.1.call-update) | async-done | bytes 262160 | tf_op jit(solution)/shard_map/reduce_scatter | solution.py:25
  356.3 1.0 convert_element_type.139
  357.2 2.7 collective-permute-start.4
  359.9 5.9 collective-permute-done.4
  365.8 1.0 fusion.28
  366.8 5.9 collective-permute-start.5
  372.7 6.4 collective-permute-done.5
  379.1 1.6 add_convert_fusion
  380.8 25.4 %all-gather.3.cloned.1.call-done = bf16[2048,256]{0,1:T(8,128)(2,1)} async-done(((bf16[256,256]{0,1:T(8,128)(2,1)}), bf16[2048,256]{0,1:T(8,128)(2,1)}) %all-gather.3.cloned.1.call-update) | async-done | bytes 1048592 | tf_op jit(solution)/shard_map/all_gather | solution.py:37
  406.2 2.6 fusion.25
  409.8 41.9 %reduce-scatter.37.cloned.1.call-done = bf16[64,256]{1,0:T(8,128)(2,1)} async-done(((bf16[512,256]{1,0:T(8,128)(2,1)}), bf16[64,256]{1,0:T(8,128)(2,1)}) %reduce-scatter.37.cloned.1.call-update) | async-done | bytes 32784 | tf_op jit(solution)/shard_map/reduce_scatter | solution.py:38
  451.7 1.4 gather_fusion.1
  453.1 5.1 collective-permute-start.6
  458.3 2.8 collective-permute-done.6
  461.1 2.5 collective-permute-start.7
  463.8 2.0 collective-permute-done.7
  466.4 28.4 %all_gather.36 = bf16[512,256]{1,0:T(8,128)(2,1)S(1)} all-gather(bf16[64,256]{1,0:T(8,128)(2,1)S(1)} %bitcast_select_fusion), channel_id=1, replica_groups=mesh['leaf'=4,'row'=8,'col'=8] {'row'}, dimensions={0}, use_global_device_ids=true | all-gather | bytes 294912 | tf_op jit(solution)/shard_map/all_gather | solution.py:24
  494.8 3.2 convolution_bitcast_fusion
  498.0 3.0 copy.51
  501.1 31.2 %reduce-scatter.39.cloned.1.call-done = f32[192,256]{1,0:T(8,128)} async-done(((f32[1536,256]{1,0:T(8,128)}), f32[192,256]{1,0:T(8,128)}) %reduce-scatter.39.cloned.1.call-update) | async-done | bytes 196624
  532.3 1.1 copy.52
  533.4 2.6 collective-permute-start.8
  536.0 5.8 collective-permute-done.8
  541.9 14.6 %all_gather.37 = bf16[1536,256]{1,0:T(8,128)(2,1)S(1)} all-gather(bf16[192,256]{1,0:T(8,128)(2,1)S(1)} %copy.38), channel_id=1, replica_groups=mesh['leaf'=4,'row'=8,'col'=8] {'col'}, dimensions={0}, use_global_device_ids=true | all-gather | bytes 884736 | tf_op jit(solution)/shard_map/all_gather | solution.py:37
  558.4 42.1 %reduce-scatter.41.cloned.1.call-done = bf16[96,256]{1,0:T(8,128)(2,1)} async-done(((bf16[768,256]{1,0:T(8,128)(2,1)}), bf16[96,256]{1,0:T(8,128)(2,1)}) %reduce-scatter.41.cloned.1.call-update) | async-done | bytes 49168 | tf_op jit(solution)/shard_map/reduce_scatter | solution.py:38
  601.9 2.6 collective-permute-start.9
  605.2 1.8 collective-permute-done.9
  607.1 29.0 %all_gather.38 = bf16[1024,256]{1,0:T(8,128)(2,1)S(1)} all-gather(bf16[128,256]{1,0:T(8,128)(2,1)S(1)} %fusion.29), channel_id=1, replica_groups=mesh['leaf'=4,'row'=8,'col'=8] {'row'}, dimensions={0}, use_global_device_ids=true | all-gather | bytes 589824 | tf_op jit(solution)/shard_map/all_gather | solution.py:24
  636.1 3.3 fusion.8
  639.5 30.3 %reduce-scatter.29.cloned.1.call-done = f32[128,256]{1,0:T(8,128)} async-done(((f32[1024,256]{1,0:T(8,128)}), f32[128,256]{1,0:T(8,128)}) %reduce-scatter.29.cloned.1.call-update) | async-done | bytes 131088 | tf_op jit(solution)/shard_map/reduce_scatter | solution.py:25
  670.6 13.7 %all_gather.39 = bf16[1024,256]{1,0:T(8,128)(2,1)S(1)} all-gather(bf16[128,256]{1,0:T(8,128)(2,1)S(1)} %subtract_convert_fusion.1), channel_id=1, replica_groups=mesh['leaf'=4,'row'=8,'col'=8] {'col'}, dimensions={0}, use_global_device_ids=true | all-gather | bytes 589824 | tf_op jit(solution)/shard_map/all_gather | solution.py:37
  684.4 2.3 fusion.20
  686.7 1.0 copy.55
  689.0 41.8 %reduce-scatter.43.cloned.1.call-done = bf16[128,256]{1,0:T(8,128)(2,1)} async-done(((bf16[1024,256]{1,0:T(8,128)(2,1)}), bf16[128,256]{1,0:T(8,128)(2,1)}) %reduce-scatter.43.cloned.1.call-update) | async-done | bytes 65552
  730.8 0.9 copy.56
  (94 shorter events, 13.8 us)
Async XLA Ops:
  7.2 165.0 %copy-start = (bf16[1536,768]{1,0:T(8,128)(2,1)S(1)}, bf16[1536,768]{1,0:T(8,128)(2,1)}, u32[]{:S(2)}) copy-start(bf16[1536,768]{1,0:T(8,128)(2,1)} %param.15) | copy-start | bytes 7077892
  7.2 67.9 %reduce-scatter.25.cloned.1.call-start = ((), (), s32[]{:S(2)}) async-start(), calls=%async_computation.10 | async-start | bytes 1179648 | tf_op jit(solution)/shard_map/reduce_scatter | solution.py:25
  41.4 94.8 %reduce-scatter.31.cloned.1.call-start = ((), (), s32[]{:S(2)}) async-start(), calls=%async_computation.14 | async-start | bytes 589824 | tf_op jit(solution)/shard_map/reduce_scatter | solution.py:38
  89.8 3.5 copy-start.7
  89.8 50.1 %copy-start.5 = (f32[1,1,1,96,256]{4,3,2,1,0:T(8,128)S(1)}, f32[1,1,1,96,256]{4,3,2,1,0:T(8,128)}, u32[]{:S(2)}) copy-start(f32[1,1,1,96,256]{4,3,2,1,0:T(8,128)} %param.11) | copy-start | bytes 294916
  93.2 115.1 %reduce-scatter.33.cloned.1.call-start = ((), (), s32[]{:S(2)}) async-start(), calls=%async_computation.15 | async-start | bytes 1769472
  137.1 5.2 collective-permute-start
  177.2 100.2 %reduce-scatter.35.cloned.1.call-start = ((), (), s32[]{:S(2)}) async-start(), calls=%async_computation.16 | async-start | bytes 294912 | tf_op jit(solution)/shard_map/reduce_scatter | solution.py:38
  209.3 8.4 %collective-permute-start.1 = (bf16[192,256]{0,1:T(8,128)(2,1)S(1)}, bf16[192,256]{0,1:T(8,128)(2,1)S(1)}, u32[]{:S(2)}, u32[]{:S(2)}) collective-permute-start(bf16[192,256]{0,1:T(8,128)(2,1)S(1)} %convert_element_type.131), channel_id=1, source_target_pairs={{0,64},{64,0},{128,192},{192,128},{1,65},{65,1},{129,193},{193,129... | collective-permute-start | bytes 294920 | tf_op jit(solution)/shard_map/ppermute | solution.py:16
  217.9 17.6 %copy-start.6 = (s32[1,1,1,4,16]{4,3,2,1,0:T(4,128)S(1)}, s32[1,1,1,4,16]{4,3,2,1,0:T(4,128)}, u32[]{:S(2)}) copy-start(s32[1,1,1,4,16]{4,3,2,1,0:T(4,128)} %param.19) | copy-start | bytes 772
  232.5 58.2 %copy-start.1 = (f32[1,1,1,64,256]{4,3,2,1,0:T(8,128)S(1)}, f32[1,1,1,64,256]{4,3,2,1,0:T(8,128)}, u32[]{:S(2)}) copy-start(f32[1,1,1,64,256]{4,3,2,1,0:T(8,128)} %param.12) | copy-start | bytes 196612
  235.4 120.9 %reduce-scatter.27.cloned.1.call-start = ((), (), s32[]{:S(2)}) async-start(), calls=%async_computation.11 | async-start | bytes 2359296 | tf_op jit(solution)/shard_map/reduce_scatter | solution.py:25
  278.2 4.8 collective-permute-start.2
  283.0 7.7 %collective-permute-start.3 = (bf16[2,16,256]{2,1,0:T(8,128)(2,1)S(1)}, bf16[2,16,256]{2,1,0:T(8,128)(2,1)S(1)}, u32[]{:S(2)}, u32[]{:S(2)}) collective-permute-start(bf16[2,16,256]{2,1,0:T(8,128)(2,1)S(1)} %pad_maximum_fusion.4), channel_id=1, source_target_pairs={{0,128},{128,0},{64,192},{192,64},{1,129},{129,1},{65,193},{193,65... | collective-permute-start | bytes 49160 | tf_op jit(solution)/shard_map/ppermute | solution.py:16
  323.9 82.4 %all-gather.3.cloned.1.call-start = ((), (), s32[]{:S(2)}) async-start(), calls=%async_computation.12 | async-start | bytes 1179648 | tf_op jit(solution)/shard_map/all_gather | solution.py:37
  357.2 8.6 %collective-permute-start.4 = (bf16[256,256]{0,1:T(8,128)(2,1)S(1)}, bf16[256,256]{0,1:T(8,128)(2,1)S(1)}, u32[]{:S(2)}, u32[]{:S(2)}) collective-permute-start(bf16[256,256]{0,1:T(8,128)(2,1)S(1)} %convert_element_type.139), channel_id=1, source_target_pairs={{0,64},{64,0},{128,192},{192,128},{1,65},{65,1},{129,193},{193,129... | collective-permute-start | bytes 393224 | tf_op jit(solution)/shard_map/ppermute | solution.py:16
  366.8 12.3 %collective-permute-start.5 = (bf16[256,256]{0,1:T(8,128)(2,1)S(1)}, bf16[256,256]{0,1:T(8,128)(2,1)S(1)}, u32[]{:S(2)}, u32[]{:S(2)}) collective-permute-start(bf16[256,256]{0,1:T(8,128)(2,1)S(1)} %fusion.28), channel_id=1, source_target_pairs={{0,128},{128,0},{64,192},{192,64},{1,129},{129,1},{65,193},{193,65... | collective-permute-start | bytes 393224 | tf_op jit(solution)/shard_map/ppermute | solution.py:16
  380.7 71.0 %reduce-scatter.37.cloned.1.call-start = ((), (), s32[]{:S(2)}) async-start(), calls=%async_computation.17 | async-start | bytes 294912 | tf_op jit(solution)/shard_map/reduce_scatter | solution.py:38
  409.7 122.6 %reduce-scatter.39.cloned.1.call-start = ((), (), s32[]{:S(2)}) async-start(), calls=%async_computation.18 | async-start | bytes 1769472
  453.1 7.9 %collective-permute-start.6 = (bf16[2,16,256]{2,1,0:T(8,128)(2,1)S(1)}, bf16[2,16,256]{2,1,0:T(8,128)(2,1)S(1)}, u32[]{:S(2)}, u32[]{:S(2)}) collective-permute-start(bf16[2,16,256]{2,1,0:T(8,128)(2,1)S(1)} %pad_maximum_fusion.5), channel_id=1, source_target_pairs={{0,128},{128,0},{64,192},{192,64},{1,129},{129,1},{65,193},{193,65... | collective-permute-start | bytes 49160 | tf_op jit(solution)/shard_map/ppermute | solution.py:16
  461.1 4.7 collective-permute-start.7
  501.1 99.4 %reduce-scatter.41.cloned.1.call-start = ((), (), s32[]{:S(2)}) async-start(), calls=%async_computation.19 | async-start | bytes 442368 | tf_op jit(solution)/shard_map/reduce_scatter | solution.py:38
  533.4 8.4 %collective-permute-start.8 = (bf16[192,256]{0,1:T(8,128)(2,1)S(1)}, bf16[192,256]{0,1:T(8,128)(2,1)S(1)}, u32[]{:S(2)}, u32[]{:S(2)}) collective-permute-start(bf16[192,256]{0,1:T(8,128)(2,1)S(1)} %convert_element_type.149), channel_id=1, source_target_pairs={{0,64},{64,0},{128,192},{192,128},{1,65},{65,1},{129,193},{193,129... | collective-permute-start | bytes 294920 | tf_op jit(solution)/shard_map/ppermute | solution.py:16
  558.3 111.4 %reduce-scatter.29.cloned.1.call-start = ((), (), s32[]{:S(2)}) async-start(), calls=%async_computation.13 | async-start | bytes 1179648 | tf_op jit(solution)/shard_map/reduce_scatter | solution.py:25
  601.9 5.1 collective-permute-start.9
  636.1 33.7 %copy-start.3 = (f32[128,256]{1,0:T(8,128)S(1)}, f32[128,256]{1,0:T(8,128)}, u32[]{:S(2)}) copy-start(f32[128,256]{1,0:T(8,128)} %reduce-scatter.25.cloned.1.call-done) | copy-start | bytes 393220
  639.4 91.4 %reduce-scatter.43.cloned.1.call-start = ((), (), s32[]{:S(2)}) async-start(), calls=%async_computation.20 | async-start | bytes 589824
  684.4 3.4 copy-start.2
  684.4 4.0 copy-start.4
Sparse Core Ops, SparseCore 0:
  41.6 33.4 reduce-scatter.24
  93.3 42.8 reduce-scatter.30
  177.3 30.8 reduce-scatter.32
  235.5 41.8 reduce-scatter.34
  324.0 32.2 reduce-scatter.26
  380.9 25.3 all-gather.2
  409.8 41.8 reduce-scatter.36
  501.2 31.0 reduce-scatter.38
  558.4 41.9 reduce-scatter.40
  639.5 30.1 reduce-scatter.28
  687.9 42.9 reduce-scatter.42
where the time goes:
time: 740 us; the launch traced here: 739 us
  waiting for transfers between devices  431 us (58%)
  blocking collectives  201 us (27%)
  starting transfers between devices  34.8 us (5%)
  matrix products  25.6 us (3%)
  local copies, waits for them, and re-layouts  19 us (3%)
  between operations  14.2 us (2%)
  other arithmetic  13.7 us (2%)
    reduce_scatter x4, waiting for transfers between devices, reverse_apply(): lax.psum_scatter(lax.dot_general(matrix, gathered, (((0,), (0,)), ((), ()...  168 us
    all_gather x5, blocking collectives, forward_apply(): gathered = lax.all_gather(vector, 'row', axis=0, tiled=True)  144 us
    unnamed x14, waiting for transfers between devices  104 us
    reduce_scatter x3, waiting for transfers between devices, forward_apply(): lax.psum_scatter(jnp.dot(matrix, gathered, preferred_element_type=jnp.flo...  96.2 us
    all_gather x4, blocking collectives, reverse_apply(): gathered = lax.all_gather(vector, 'col', axis=0, tiled=True)  56.7 us
    ppermute x10, waiting for transfers between devices, from_partner(): return lax.ppermute(block, axis, route)  36.8 us
    ppermute x10, starting transfers between devices, from_partner(): return lax.ppermute(block, axis, route)  34.3 us
    all_gather x1, waiting for transfers between devices, reverse_apply(): gathered = lax.all_gather(vector, 'col', axis=0, tiled=True)  25.4 us
  transfers between devices with their start and end apart: 21, of which 21 were waited for; matrix products, arithmetic and copies ran while one was open for 1% of the time, Pallas kernels for 0%

commit v1 on v0

--- a/solution.py
+++ b/solution.py
@@ -21,7 +21,9 @@
 
 
 def forward_apply(matrix, vector, leaf_bits):
-    gathered = lax.all_gather(vector, "row", axis=0, tiled=True)
+    gathered = jnp.concatenate(
+        lax.all_to_all(jnp.stack([vector] * lax.axis_size("row")), "row", 0, 0), axis=0
+    )
     result = lax.psum_scatter(
         jnp.dot(matrix, gathered, preferred_element_type=jnp.float32),
         "col",

time: 740 us -> 650 us (0.88)
  blocking collectives: 201 us -> 113 us
    all_gather x5 -> x0, blocking collectives: 144 us -> none  [forward_apply(): gathered = lax.all_gather(vector, 'row', axis=0, tiled=True)]
    all_to_all x0 -> x5, blocking collectives: none -> 56.7 us  [forward_apply(): lax.all_to_all(jnp.stack([vector] * lax.axis_size('row')), 'row', 0, 0)]
where the time goes in v1:
time: 650 us; the launch traced here: 649 us
  waiting for transfers between devices  428 us (66%)
  blocking collectives  113 us (17%)
  starting transfers between devices  34.8 us (5%)
  matrix products  25.6 us (4%)
  local copies, waits for them, and re-layouts  19.1 us (3%)
  between operations  14.3 us (2%)
  other arithmetic  13.7 us (2%)
    reduce_scatter x4, waiting for transfers between devices, reverse_apply(): lax.psum_scatter(lax.dot_general(matrix, gathered, (((0,), (0,)), ((), ()...  168 us
    unnamed x14, waiting for transfers between devices  104 us
    reduce_scatter x3, waiting for transfers between devices, forward_apply(): lax.psum_scatter(jnp.dot(matrix, gathered, preferred_element_type=jnp.flo...  93.4 us
    all_gather x4, blocking collectives, reverse_apply(): gathered = lax.all_gather(vector, 'col', axis=0, tiled=True)  56.8 us
    all_to_all x5, blocking collectives, forward_apply(): lax.all_to_all(jnp.stack([vector] * lax.axis_size('row')), 'row', 0, 0)  56.7 us
    ppermute x10, waiting for transfers between devices, from_partner(): return lax.ppermute(block, axis, route)  36.9 us
    ppermute x10, starting transfers between devices, from_partner(): return lax.ppermute(block, axis, route)  34.4 us
    all_gather x1, waiting for transfers between devices, reverse_apply(): gathered = lax.all_gather(vector, 'col', axis=0, tiled=True)  25.4 us
  transfers between devices with their start and end apart: 21, of which 21 were waited for; matrix products, arithmetic and copies ran while one was open for 1% of the time, Pallas kernels for 0%

profile of v1, /device:TPU:2, one launch (start us, length us, event | category | flops | bytes accessed | tf_op | source)
XLA Modules:
  0.0 648.8 jit_solution(7357442035881450778)
XLA Ops:
  7.2 1.1 convert_bitcast_fusion
  8.3 15.7 %all_to_all.25 = bf16[8,128,256]{2,1,0:T(8,128)(2,1)S(1)} all-to-all(bf16[8,128,256]{2,1,0:T(8,128)(2,1)S(1)} %stack.27), channel_id=1, replica_groups=mesh['leaf'=4,'row'=8,'col'=8] {'row'}, dimensions={0} | all-to-all | bytes 1048576 | tf_op jit(solution)/shard_map/all_to_all | solution.py:25
  24.0 3.3 fusion.6
  27.4 31.6 %reduce-scatter.25.cloned.1.call-done = f32[128,256]{1,0:T(8,128)} async-done(((f32[1024,256]{1,0:T(8,128)}), f32[128,256]{1,0:T(8,128)}) %reduce-scatter.25.cloned.1.call-update) | async-done | bytes 131088 | tf_op jit(solution)/shard_map/reduce_scatter | solution.py:27
  59.9 13.8 %all_gather.15 = bf16[1024,256]{1,0:T(8,128)(2,1)S(1)} all-gather(bf16[128,256]{1,0:T(8,128)(2,1)S(1)} %convert_element_type.131), channel_id=1, replica_groups=mesh['leaf'=4,'row'=8,'col'=8] {'col'}, dimensions={0}, use_global_device_ids=true | all-gather | bytes 589824 | tf_op jit(solution)/shard_map/all_gather | solution.py:39
  73.7 2.4 fusion.17
  76.1 1.0 copy.46
  77.2 43.0 %reduce-scatter.31.cloned.1.call-done = bf16[128,256]{1,0:T(8,128)(2,1)} async-done(((bf16[1024,256]{1,0:T(8,128)(2,1)}), bf16[128,256]{1,0:T(8,128)(2,1)}) %reduce-scatter.31.cloned.1.call-update) | async-done | bytes 65552 | tf_op jit(solution)/shard_map/reduce_scatter | solution.py:40
  121.1 2.7 collective-permute-start
  123.8 1.0 scatter_custom_fusion
  124.9 1.4 collective-permute-done
  126.3 1.0 scatter_custom_fusion.1
  127.4 10.4 %all_to_all.26 = bf16[8,96,256]{2,1,0:T(8,128)(2,1)S(1)} all-to-all(bf16[8,96,256]{2,1,0:T(8,128)(2,1)S(1)} %stack.28), channel_id=1, replica_groups=mesh['leaf'=4,'row'=8,'col'=8] {'row'}, dimensions={0} | all-to-all | bytes 786432 | tf_op jit(solution)/shard_map/all_to_all | solution.py:25
  137.7 2.0 convolution_bitcast_fusion.2
  139.7 3.0 copy.48
  142.9 31.0 %reduce-scatter.33.cloned.1.call-done = f32[192,256]{1,0:T(8,128)} async-done(((f32[1536,256]{1,0:T(8,128)}), f32[192,256]{1,0:T(8,128)}) %reduce-scatter.33.cloned.1.call-update) | async-done | bytes 196624
  173.9 1.1 copy.49
  175.0 2.7 collective-permute-start.1
  177.6 5.7 collective-permute-done.1
  183.5 14.6 %all_gather.16 = bf16[1536,256]{1,0:T(8,128)(2,1)S(1)} all-gather(bf16[192,256]{1,0:T(8,128)(2,1)S(1)} %copy.38), channel_id=1, replica_groups=mesh['leaf'=4,'row'=8,'col'=8] {'col'}, dimensions={0}, use_global_device_ids=true | all-gather | bytes 884736 | tf_op jit(solution)/shard_map/all_gather | solution.py:39
  198.1 2.0 fusion.24
  201.8 41.1 %reduce-scatter.35.cloned.1.call-done = bf16[64,256]{1,0:T(8,128)(2,1)} async-done(((bf16[512,256]{1,0:T(8,128)(2,1)}), bf16[64,256]{1,0:T(8,128)(2,1)}) %reduce-scatter.35.cloned.1.call-update) | async-done | bytes 32784 | tf_op jit(solution)/shard_map/reduce_scatter | solution.py:40
  243.7 2.6 collective-permute-start.2
  246.3 2.2 collective-permute-done.2
  248.5 4.9 collective-permute-start.3
  253.4 2.9 collective-permute-done.3
  256.3 1.0 scatter_fusion
  257.3 9.9 %all_to_all.27 = bf16[8,64,256]{2,1,0:T(8,128)(2,1)S(1)} all-to-all(bf16[8,64,256]{2,1,0:T(8,128)(2,1)S(1)} %stack.32), channel_id=1, replica_groups=mesh['leaf'=4,'row'=8,'col'=8] {'row'}, dimensions={0} | all-to-all | bytes 524288 | tf_op jit(solution)/shard_map/all_to_all | solution.py:25
  267.2 3.7 convolution_bitcast_fusion.1
  271.0 31.6 %reduce-scatter.27.cloned.1.call-done = f32[256,256]{0,1:T(8,128)} async-done(((f32[2048,256]{0,1:T(8,128)}), f32[256,256]{0,1:T(8,128)}) %reduce-scatter.27.cloned.1.call-update) | async-done | bytes 262160 | tf_op jit(solution)/shard_map/reduce_scatter | solution.py:27
  302.6 1.0 convert_element_type.145
  303.5 2.6 collective-permute-start.4
  306.2 5.9 collective-permute-done.4
  312.1 1.0 fusion.27
  313.1 5.9 collective-permute-start.5
  319.0 6.4 collective-permute-done.5
  325.4 1.6 add_convert_fusion
  327.1 25.4 %all-gather.2.cloned.1.call-done = bf16[2048,256]{0,1:T(8,128)(2,1)} async-done(((bf16[256,256]{0,1:T(8,128)(2,1)}), bf16[2048,256]{0,1:T(8,128)(2,1)}) %all-gather.2.cloned.1.call-update) | async-done | bytes 1048592 | tf_op jit(solution)/shard_map/all_gather | solution.py:39
  352.5 2.6 fusion.25
  356.0 41.9 %reduce-scatter.37.cloned.1.call-done = bf16[64,256]{1,0:T(8,128)(2,1)} async-done(((bf16[512,256]{1,0:T(8,128)(2,1)}), bf16[64,256]{1,0:T(8,128)(2,1)}) %reduce-scatter.37.cloned.1.call-update) | async-done | bytes 32784 | tf_op jit(solution)/shard_map/reduce_scatter | solution.py:40
  398.0 1.4 gather_fusion.1
  399.4 5.1 collective-permute-start.6
  404.6 2.8 collective-permute-done.6
  407.3 2.5 collective-permute-start.7
  410.0 2.0 collective-permute-done.7
  412.7 9.7 %all_to_all.28 = bf16[8,64,256]{2,1,0:T(8,128)(2,1)S(1)} all-to-all(bf16[8,64,256]{2,1,0:T(8,128)(2,1)S(1)} %stack.36), channel_id=1, replica_groups=mesh['leaf'=4,'row'=8,'col'=8] {'row'}, dimensions={0} | all-to-all | bytes 524288 | tf_op jit(solution)/shard_map/all_to_all | solution.py:25
  422.4 3.2 convolution_bitcast_fusion
  425.6 3.0 copy.54
  428.7 31.0 %reduce-scatter.39.cloned.1.call-done = f32[192,256]{1,0:T(8,128)} async-done(((f32[1536,256]{1,0:T(8,128)}), f32[192,256]{1,0:T(8,128)}) %reduce-scatter.39.cloned.1.call-update) | async-done | bytes 196624
  459.7 1.1 copy.55
  460.8 2.6 collective-permute-start.8
  463.4 5.7 collective-permute-done.8
  469.3 14.6 %all_gather.18 = bf16[1536,256]{1,0:T(8,128)(2,1)S(1)} all-gather(bf16[192,256]{1,0:T(8,128)(2,1)S(1)} %copy.41), channel_id=1, replica_groups=mesh['leaf'=4,'row'=8,'col'=8] {'col'}, dimensions={0}, use_global_device_ids=true | all-gather | bytes 884736 | tf_op jit(solution)/shard_map/all_gather | solution.py:39
  485.7 42.2 %reduce-scatter.41.cloned.1.call-done = bf16[96,256]{1,0:T(8,128)(2,1)} async-done(((bf16[768,256]{1,0:T(8,128)(2,1)}), bf16[96,256]{1,0:T(8,128)(2,1)}) %reduce-scatter.41.cloned.1.call-update) | async-done | bytes 49168 | tf_op jit(solution)/shard_map/reduce_scatter | solution.py:40
  529.5 2.7 collective-permute-start.9
  532.8 1.9 collective-permute-done.9
  534.8 11.0 %all_to_all.29 = bf16[8,128,256]{2,1,0:T(8,128)(2,1)S(1)} all-to-all(bf16[8,128,256]{2,1,0:T(8,128)(2,1)S(1)} %stack.37), channel_id=1, replica_groups=mesh['leaf'=4,'row'=8,'col'=8] {'row'}, dimensions={0} | all-to-all | bytes 1048576 | tf_op jit(solution)/shard_map/all_to_all | solution.py:25
  545.8 3.3 fusion.8
  549.2 30.2 %reduce-scatter.29.cloned.1.call-done = f32[128,256]{1,0:T(8,128)} async-done(((f32[1024,256]{1,0:T(8,128)}), f32[128,256]{1,0:T(8,128)}) %reduce-scatter.29.cloned.1.call-update) | async-done | bytes 131088 | tf_op jit(solution)/shard_map/reduce_scatter | solution.py:27
  580.3 13.8 %all_gather.19 = bf16[1024,256]{1,0:T(8,128)(2,1)S(1)} all-gather(bf16[128,256]{1,0:T(8,128)(2,1)S(1)} %subtract_convert_fusion.1), channel_id=1, replica_groups=mesh['leaf'=4,'row'=8,'col'=8] {'col'}, dimensions={0}, use_global_device_ids=true | all-gather | bytes 589824 | tf_op jit(solution)/shard_map/all_gather | solution.py:39
  594.1 2.3 fusion.20
  596.4 1.0 copy.58
  598.8 41.8 %reduce-scatter.43.cloned.1.call-done = bf16[128,256]{1,0:T(8,128)(2,1)} async-done(((bf16[1024,256]{1,0:T(8,128)(2,1)}), bf16[128,256]{1,0:T(8,128)(2,1)}) %reduce-scatter.43.cloned.1.call-update) | async-done | bytes 65552
  640.5 0.9 copy.59
  (99 shorter events, 13.9 us)
Async XLA Ops:
  7.2 130.6 %copy-start = (bf16[1536,768]{1,0:T(8,128)(2,1)S(1)}, bf16[1536,768]{1,0:T(8,128)(2,1)}, u32[]{:S(2)}) copy-start(bf16[1536,768]{1,0:T(8,128)(2,1)} %param.15) | copy-start | bytes 7077892
  7.2 51.8 %reduce-scatter.25.cloned.1.call-start = ((), (), s32[]{:S(2)}) async-start(), calls=%async_computation.15 | async-start | bytes 1179648 | tf_op jit(solution)/shard_map/reduce_scatter | solution.py:27
  27.3 92.9 %reduce-scatter.31.cloned.1.call-start = ((), (), s32[]{:S(2)}) async-start(), calls=%async_computation.19 | async-start | bytes 589824 | tf_op jit(solution)/shard_map/reduce_scatter | solution.py:40
  73.7 3.5 copy-start.7
  73.7 50.1 %copy-start.5 = (f32[1,1,1,96,256]{4,3,2,1,0:T(8,128)S(1)}, f32[1,1,1,96,256]{4,3,2,1,0:T(8,128)}, u32[]{:S(2)}) copy-start(f32[1,1,1,96,256]{4,3,2,1,0:T(8,128)} %param.11) | copy-start | bytes 294916
  77.1 96.8 %reduce-scatter.33.cloned.1.call-start = ((), (), s32[]{:S(2)}) async-start(), calls=%async_computation.20 | async-start | bytes 1769472
  121.1 5.2 collective-permute-start
  142.8 100.2 %reduce-scatter.35.cloned.1.call-start = ((), (), s32[]{:S(2)}) async-start(), calls=%async_computation.21 | async-start | bytes 294912 | tf_op jit(solution)/shard_map/reduce_scatter | solution.py:40
  175.0 8.4 %collective-permute-start.1 = (bf16[192,256]{0,1:T(8,128)(2,1)S(1)}, bf16[192,256]{0,1:T(8,128)(2,1)S(1)}, u32[]{:S(2)}, u32[]{:S(2)}) collective-permute-start(bf16[192,256]{0,1:T(8,128)(2,1)S(1)} %convert_element_type.137), channel_id=1, source_target_pairs={{0,64},{64,0},{128,192},{192,128},{1,65},{65,1},{129,193},{193,129... | collective-permute-start | bytes 294920 | tf_op jit(solution)/shard_map/ppermute | solution.py:16
  183.5 17.6 %copy-start.6 = (s32[1,1,1,4,16]{4,3,2,1,0:T(4,128)S(1)}, s32[1,1,1,4,16]{4,3,2,1,0:T(4,128)}, u32[]{:S(2)}) copy-start(s32[1,1,1,4,16]{4,3,2,1,0:T(4,128)} %param.19) | copy-start | bytes 772
  198.1 58.1 %copy-start.1 = (f32[1,1,1,64,256]{4,3,2,1,0:T(8,128)S(1)}, f32[1,1,1,64,256]{4,3,2,1,0:T(8,128)}, u32[]{:S(2)}) copy-start(f32[1,1,1,64,256]{4,3,2,1,0:T(8,128)} %param.12) | copy-start | bytes 196612
  201.0 101.5 %reduce-scatter.27.cloned.1.call-start = ((), (), s32[]{:S(2)}) async-start(), calls=%async_computation.16 | async-start | bytes 2359296 | tf_op jit(solution)/shard_map/reduce_scatter | solution.py:27
  243.7 4.8 collective-permute-start.2
  248.5 7.7 %collective-permute-start.3 = (bf16[2,16,256]{2,1,0:T(8,128)(2,1)S(1)}, bf16[2,16,256]{2,1,0:T(8,128)(2,1)S(1)}, u32[]{:S(2)}, u32[]{:S(2)}) collective-permute-start(bf16[2,16,256]{2,1,0:T(8,128)(2,1)S(1)} %pad_maximum_fusion.4), channel_id=1, source_target_pairs={{0,128},{128,0},{64,192},{192,64},{1,129},{129,1},{65,193},{193,65... | collective-permute-start | bytes 49160 | tf_op jit(solution)/shard_map/ppermute | solution.py:16
  270.9 81.6 %all-gather.2.cloned.1.call-start = ((), (), s32[]{:S(2)}) async-start(), calls=%async_computation.17 | async-start | bytes 1179648 | tf_op jit(solution)/shard_map/all_gather | solution.py:39
  303.5 8.6 %collective-permute-start.4 = (bf16[256,256]{0,1:T(8,128)(2,1)S(1)}, bf16[256,256]{0,1:T(8,128)(2,1)S(1)}, u32[]{:S(2)}, u32[]{:S(2)}) collective-permute-start(bf16[256,256]{0,1:T(8,128)(2,1)S(1)} %convert_element_type.145), channel_id=1, source_target_pairs={{0,64},{64,0},{128,192},{192,128},{1,65},{65,1},{129,193},{193,129... | collective-permute-start | bytes 393224 | tf_op jit(solution)/shard_map/ppermute | solution.py:16
  313.1 12.3 %collective-permute-start.5 = (bf16[256,256]{0,1:T(8,128)(2,1)S(1)}, bf16[256,256]{0,1:T(8,128)(2,1)S(1)}, u32[]{:S(2)}, u32[]{:S(2)}) collective-permute-start(bf16[256,256]{0,1:T(8,128)(2,1)S(1)} %fusion.27), channel_id=1, source_target_pairs={{0,128},{128,0},{64,192},{192,64},{1,129},{129,1},{65,193},{193,65... | collective-permute-start | bytes 393224 | tf_op jit(solution)/shard_map/ppermute | solution.py:16
  327.1 70.9 %reduce-scatter.37.cloned.1.call-start = ((), (), s32[]{:S(2)}) async-start(), calls=%async_computation.22 | async-start | bytes 294912 | tf_op jit(solution)/shard_map/reduce_scatter | solution.py:40
  356.0 103.7 %reduce-scatter.39.cloned.1.call-start = ((), (), s32[]{:S(2)}) async-start(), calls=%async_computation.23 | async-start | bytes 1769472
  399.4 7.9 %collective-permute-start.6 = (bf16[2,16,256]{2,1,0:T(8,128)(2,1)S(1)}, bf16[2,16,256]{2,1,0:T(8,128)(2,1)S(1)}, u32[]{:S(2)}, u32[]{:S(2)}) collective-permute-start(bf16[2,16,256]{2,1,0:T(8,128)(2,1)S(1)} %pad_maximum_fusion.5), channel_id=1, source_target_pairs={{0,128},{128,0},{64,192},{192,64},{1,129},{129,1},{65,193},{193,65... | collective-permute-start | bytes 49160 | tf_op jit(solution)/shard_map/ppermute | solution.py:16
  407.3 4.7 collective-permute-start.7
  428.7 99.3 %reduce-scatter.41.cloned.1.call-start = ((), (), s32[]{:S(2)}) async-start(), calls=%async_computation.24 | async-start | bytes 442368 | tf_op jit(solution)/shard_map/reduce_scatter | solution.py:40
  460.8 8.4 %collective-permute-start.8 = (bf16[192,256]{0,1:T(8,128)(2,1)S(1)}, bf16[192,256]{0,1:T(8,128)(2,1)S(1)}, u32[]{:S(2)}, u32[]{:S(2)}) collective-permute-start(bf16[192,256]{0,1:T(8,128)(2,1)S(1)} %convert_element_type.155), channel_id=1, source_target_pairs={{0,64},{64,0},{128,192},{192,128},{1,65},{65,1},{129,193},{193,129... | collective-permute-start | bytes 294920 | tf_op jit(solution)/shard_map/ppermute | solution.py:16
  485.7 93.7 %reduce-scatter.29.cloned.1.call-start = ((), (), s32[]{:S(2)}) async-start(), calls=%async_computation.18 | async-start | bytes 1179648 | tf_op jit(solution)/shard_map/reduce_scatter | solution.py:27
  529.5 5.3 collective-permute-start.9
  545.8 33.6 %copy-start.3 = (f32[128,256]{1,0:T(8,128)S(1)}, f32[128,256]{1,0:T(8,128)}, u32[]{:S(2)}) copy-start(f32[128,256]{1,0:T(8,128)} %reduce-scatter.25.cloned.1.call-done) | copy-start | bytes 393220
  549.2 91.4 %reduce-scatter.43.cloned.1.call-start = ((), (), s32[]{:S(2)}) async-start(), calls=%async_computation.25 | async-start | bytes 589824
  594.1 3.4 copy-start.2
  594.1 4.0 copy-start.4
Sparse Core Ops, SparseCore 0:
  27.5 31.5 reduce-scatter.24
  77.2 42.9 reduce-scatter.30
  142.9 30.9 reduce-scatter.32
  201.1 41.7 reduce-scatter.34
  271.0 31.4 reduce-scatter.26
  327.2 25.2 all-gather.1
  356.1 41.8 reduce-scatter.36
  428.8 30.8 reduce-scatter.38
  485.8 42.1 reduce-scatter.40
  549.3 30.0 reduce-scatter.28
  597.6 42.9 reduce-scatter.42
